TPU v7x, 256 devices: a whole 4x4x8 slice. The times are simulated.
256 devices in a mesh: wide: 32 (over z_hi, y, core), narrow: 8 (over z_lo, x).
Axes of the slice: x: 4, y: 4, z: 8 (z_hi: 4, z_lo: 2; z = z_hi * 2 + z_lo), core: 2. Of those that a mesh axis runs over, the one named last changes fastest.
Arguments:
- residual: bfloat16 [256, 8192], P('wide'), may hold values from -60 to 60
- norm_gain: float32 [8192], replicated, may hold values from 0.1 to 1.9
- w_query: bfloat16 [8192, 8192], P('wide', 'narrow'), may hold values from -0.0625 to 0.0625
- key_projection_weight: bfloat16 [8192, 1024], P('wide', 'narrow'), may hold values from -0.0625 to 0.0625
- value_projection_weight: bfloat16 [8192, 1024], P('wide', 'narrow'), may hold values from -0.0625 to 0.0625
- w_out: bfloat16 [8192, 8192], P('narrow', 'wide'), may hold values from -0.5 to 0.5
- cache_keys: bfloat16 [256, 8, 1024, 128], P('wide', 'narrow'), may hold values from -480 to 480
- stored_values: bfloat16 [256, 8, 1024, 128], P('wide', 'narrow'), may hold values from -24 to 24
- lengths: int32 [256], P('wide'), may hold values from 1 to 1024, as said below
- w_enc: bfloat16 [8192, 65536], P('narrow', 'wide'), may hold values from -0.0625 to 0.0625
- b_enc: float32 [65536], P('wide'), may hold values from -3 to 3
- w_dec: bfloat16 [65536, 8192], P('wide', 'narrow'), may hold values from -0.0625 to 0.0625
- b_dec: float32 [8192], P('narrow'), may hold values from -3 to 3
- clamp_index: int32 [256, 8], replicated, may hold values from 0 to 65535, as said below
- clamp_value: float32 [256, 8], replicated, may hold values from 10 to 40
Outputs:
- steered: bfloat16 [256, 8192], P('wide', 'narrow')
Inputs may be any that keep to these rules, and one draw needn't show every extreme that they name: `lengths`: row 0 has all 1024 slots filled. `clamp_index`: the 8 latents of a row are distinct.
All inputs are finite; a program needn't handle non-finite values.
Results may differ from a plain program's by a relative error of at most 0.014.
The roundings to bfloat16 on the way count: a program that leaves them out, or rounds other values in their place, can miss the bound.
Values may be sent and summed in bfloat16 or wider, within the bound.
No kernel may reach another device: no remote copies, remote signals or barrier semaphores. Data moves between devices by JAX's collectives and lax.ppermute only.
A program may use at most 64 MiB of HBM per device.

v0:
```python
import math

import jax
import jax.numpy as jnp
from jax import lax
from jax.sharding import PartitionSpec as P

HEAD_WIDTH = 128


rope_base = 500000.0


def rotary(vectors, positions):
    halfway = vectors.shape[-1] // 2
    counter = jnp.arange(halfway, dtype=jnp.float32)
    inverse = rope_base ** (-2.0 * counter / vectors.shape[-1])
    angles = positions.astype(jnp.float32)[:, None] * inverse[None, :]
    cosine = jnp.cos(angles)[:, None, :]
    sine = jnp.sin(angles)[:, None, :]
    first_half = vectors[..., :halfway]
    second_half = vectors[..., halfway:]
    return jnp.concatenate(
        [first_half * cosine - second_half * sine, second_half * cosine + first_half * sine],
        axis=-1,
    )


def clamp_latents(pre_acts, latent_first, clamp_index, clamp_value):
    columns = latent_first + jnp.arange(pre_acts.shape[1], dtype=jnp.int32)
    result = jnp.maximum(pre_acts, 0.0)
    for clamp_slot in range(clamp_index.shape[1]):
        matched = columns[None, :] == clamp_index[:, clamp_slot : clamp_slot + 1]
        result = jnp.where(matched, clamp_value[:, clamp_slot : clamp_slot + 1], result)
    return result.astype(jnp.bfloat16)


def attend(queries, key_new, value_new, cache_keys, stored_values, lengths):
    local_rows, heads_here, head_size = queries.shape
    kv_here = key_new.shape[1]
    query_group_width = heads_here // kv_here
    grouped_queries = queries.reshape(local_rows, kv_here, query_group_width, head_size)
    scaling = 1.0 / math.sqrt(head_size)
    scores = (
        jnp.einsum(
            "rkgd,rkjd->rkgj", grouped_queries, cache_keys, preferred_element_type=jnp.float32
        )
        * scaling
    )
    in_range = (
        jnp.arange(cache_keys.shape[2], dtype=jnp.int32)[None, None, None, :]
        < lengths[:, None, None, None]
    )
    scores = jnp.where(in_range, scores, -jnp.inf)
    own_score = (
        jnp.einsum("rkgd,rkd->rkg", grouped_queries, key_new, preferred_element_type=jnp.float32)
        * scaling
    )
    highest = jnp.maximum(jnp.max(scores, axis=-1), own_score)
    weights = jnp.exp(scores - highest[..., None])
    own_weight = jnp.exp(own_score - highest)
    denominator = jnp.sum(weights, axis=-1) + own_weight
    probabilities = (weights / denominator[..., None]).astype(jnp.bfloat16)
    own_prob = (own_weight / denominator).astype(jnp.bfloat16)
    blended = jnp.einsum(
        "rkgj,rkjd->rkgd", probabilities, stored_values, preferred_element_type=jnp.float32
    )
    blended = (
        blended
        + own_prob.astype(jnp.float32)[..., None] * value_new.astype(jnp.float32)[:, :, None, :]
    )
    return blended.astype(jnp.bfloat16).reshape(local_rows, heads_here * head_size)


def on_device(
    residual,
    norm_gain,
    w_query,
    key_projection_weight,
    value_projection_weight,
    w_out,
    cache_keys,
    stored_values,
    lengths,
    w_enc,
    b_enc,
    w_dec,
    b_dec,
    clamp_index,
    clamp_value,
):
    stream = residual.astype(jnp.float32)
    local_rows = residual.shape[0]
    normalized_rows = (
        stream
        * lax.rsqrt(jnp.mean(stream * stream, axis=-1, keepdims=True) + 1e-05)
        * norm_gain[None, :]
    ).astype(jnp.bfloat16)
    by_feature = lax.all_to_all(normalized_rows, "wide", split_axis=1, concat_axis=0, tiled=True)
    query_width = w_query.shape[1]
    key_width = key_projection_weight.shape[1]
    row_block = by_feature
    projected = lax.psum_scatter(
        jnp.concatenate(
            [
                jnp.dot(row_block, w_query, preferred_element_type=jnp.float32),
                jnp.dot(row_block, key_projection_weight, preferred_element_type=jnp.float32),
                jnp.dot(row_block, value_projection_weight, preferred_element_type=jnp.float32),
            ],
            axis=1,
        ),
        "wide",
        scatter_dimension=0,
        tiled=True,
    )
    heads_here = query_width // HEAD_WIDTH
    kv_here = key_width // HEAD_WIDTH
    queries = rotary(
        projected[:, :query_width].reshape(local_rows, heads_here, HEAD_WIDTH), lengths
    ).astype(jnp.bfloat16)
    key_new = rotary(
        projected[:, query_width : query_width + key_width].reshape(
            local_rows, kv_here, HEAD_WIDTH
        ),
        lengths,
    ).astype(jnp.bfloat16)
    value_new = (
        projected[:, query_width + key_width :]
        .reshape(local_rows, kv_here, HEAD_WIDTH)
        .astype(jnp.bfloat16)
    )
    attended = attend(queries, key_new, value_new, cache_keys, stored_values, lengths)
    partial_out = jnp.dot(
        lax.all_gather(attended, "wide", axis=0, tiled=True),
        w_out,
        preferred_element_type=jnp.float32,
    )
    by_row = lax.all_to_all(partial_out, "wide", split_axis=0, concat_axis=1, tiled=True)
    head_total = lax.psum_scatter(by_row, "narrow", scatter_dimension=1, tiled=True)
    width_here = w_enc.shape[0]
    narrow_index = lax.axis_index("narrow")
    own_stream = lax.dynamic_slice_in_dim(stream, narrow_index * width_here, width_here, 1)
    hidden = (own_stream + head_total).astype(jnp.bfloat16)
    partial_pre = jnp.dot(
        lax.all_gather(hidden, "wide", axis=0, tiled=True),
        w_enc,
        preferred_element_type=jnp.float32,
    )
    latents_here = w_enc.shape[1]
    latent_first = lax.axis_index("wide") * latents_here
    summed_pre = lax.psum(partial_pre, "narrow")
    activations = clamp_latents(summed_pre + b_enc[None, :], latent_first, clamp_index, clamp_value)
    row_block = activations
    rebuilt = lax.psum_scatter(
        jnp.dot(row_block, w_dec, preferred_element_type=jnp.float32),
        "wide",
        scatter_dimension=0,
        tiled=True,
    )
    return (rebuilt + b_dec[None, :]).astype(jnp.bfloat16)


def solution(mesh):
    placed = (
        P("wide", None),
        P(),
        P("wide", "narrow"),
        P("wide", "narrow"),
        P("wide", "narrow"),
        P("narrow", "wide"),
        P("wide", "narrow", None, None),
        P("wide", "narrow", None, None),
        P("wide"),
        P("narrow", "wide"),
        P("wide"),
        P("wide", "narrow"),
        P("narrow"),
        P(),
        P(),
    )
    return jax.shard_map(
        on_device, mesh=mesh, in_specs=placed, out_specs=P("wide", "narrow"), check_vma=False
    )
```

profile of v0, /device:TPU:1, one launch (start us, length us, event | category | flops | bytes accessed | tf_op | source)
XLA Modules:
  0.0 457.7 jit_solution(15226275381327403887)
XLA Ops:
  6.5 0.0 copy-start
  6.5 0.0 reduce-scatter.4.cloned.1.call-start
  6.5 1.2 multiply_reduce_fusion
  7.8 1.0 multiply_convert_fusion
  8.8 23.5 %all_to_all.38 = bf16[8,32,256]{2,0,1:T(8,128)(2,1)S(1)} all-to-all(bf16[8,32,256]{2,0,1:T(8,128)(2,1)S(1)} %bitcast.75), channel_id=1, replica_groups=mesh['wide'=32,'narrow'=8] {'wide'}, dimensions={1} | all-to-all | bytes 262144 | tf_op jit(solution)/shard_map/all_to_all | solution.py:99
  32.3 1.3 fusion.44
  33.7 0.0 copy-done.4
  33.7 0.2 fusion.40
  33.9 0.0 copy-done.5
  33.9 0.0 copy-start.9
  33.9 0.2 fusion.42
  34.1 1.2 pad_maximum_fusion
  35.3 0.0 reduce-scatter.4.cloned.1.call-update
  35.3 0.0 reduce-scatter.6.cloned.1.call-start
  35.3 0.0 copy-done.9
  35.4 0.1 iota_compare_fusion
  35.5 0.1 multiply_cosine_fusion.1
  35.6 82.7 %reduce-scatter.4.cloned.1.call-done = f32[8,1280]{1,0:T(8,128)} async-done(((f32[256,1280]{1,0:T(8,128)}), f32[8,1280]{1,0:T(8,128)}) %reduce-scatter.4.cloned.1.call-update) | async-done | bytes 40976 | tf_op jit(solution)/shard_map/reduce_scatter | solution.py:103
  118.2 0.9 slice_bitcast_fusion
  119.2 0.1 fusion.66
  119.2 0.7 slice_bitcast_fusion.1
  119.9 0.1 fusion.61
  120.0 0.1 maximum_bitcast_fusion
  120.1 0.2 fusion.56
  120.3 0.0 copy-done
  120.3 0.8 fusion.69
  121.1 0.2 fusion.39
  121.3 0.7 fusion.59
  122.0 0.4 fusion.16
  122.5 46.6 %all_gather.6 = bf16[256,1024]{1,0:T(8,128)(2,1)S(1)} all-gather(bf16[8,1024]{1,0:T(8,128)(2,1)S(1)} %bitcast.76), channel_id=1, replica_groups=mesh['wide'=32,'narrow'=8] {'wide'}, dimensions={0}, use_global_device_ids=true | all-gather | bytes 540672 | tf_op jit(solution)/shard_map/all_gather | solution.py:134
  169.1 0.3 convolution_bitcast_fusion
  169.4 18.1 %all_to_all.39 = f32[32,8,256]{2,1,0:T(8,128)} all-to-all(f32[32,8,256]{2,1,0:T(8,128)S(1)} %convolution_bitcast_fusion), channel_id=1, replica_groups=mesh['wide'=32,'narrow'=8] {'wide'}, dimensions={0} | all-to-all | bytes 524288 | tf_op jit(solution)/shard_map/all_to_all | solution.py:138
  187.6 0.0 reduce-scatter.6.cloned.1.call-update
  187.6 0.0 all-reduce.2.cloned.1.call-start
  187.6 0.0 copy-done.2
  187.7 30.0 %reduce-scatter.6.cloned.1.call-done = f32[8,1024]{1,0:T(8,128)} async-done(((f32[8,8192]{1,0:T(8,128)}), f32[8,1024]{1,0:T(8,128)}) %reduce-scatter.6.cloned.1.call-update) | async-done | bytes 32784 | tf_op jit(solution)/shard_map/reduce_scatter | solution.py:139
  217.7 0.8 add_convert_fusion.1
  218.4 51.9 %all_gather.7 = bf16[256,1024]{1,0:T(8,128)(2,1)S(1)} all-gather(bf16[8,1024]{1,0:T(8,128)(2,1)S(1)} %add_convert_fusion.1), channel_id=1, replica_groups=mesh['wide'=32,'narrow'=8] {'wide'}, dimensions={0}, use_global_device_ids=true | all-gather | bytes 540672 | tf_op jit(solution)/shard_map/all_gather | solution.py:145
  270.3 4.8 %fusion.70 = f32[256,2048]{1,0:T(8,128)} fusion(bf16[256,1024]{1,0:T(8,128)(2,1)S(1)} %all_gather.7, bf16[1024,2048]{1,0:T(8,128)(2,1)} %param.24), kind=kOutput, calls=%fused_computation.88 | convolution fusion | flops 1073741824 | bytes 6815744 | tf_op jit(solution)/shard_map/dot_general | solution.py:144
  275.1 0.0 all-reduce.2.cloned.1.call-update
  275.1 0.0 reduce-scatter.8.cloned.1.call-start
  275.2 0.6 copy-done.6
  275.8 0.0 copy-done.7
  275.8 76.3 %all-reduce.2.cloned.1.call-done = f32[256,2048]{1,0:T(8,128)} async-done(((f32[256,2048]{1,0:T(8,128)}), f32[256,2048]{1,0:T(8,128)}) %all-reduce.2.cloned.1.call-update) | async-done | bytes 2097168 | tf_op jit(solution)/shard_map/psum | solution.py:151
  352.1 6.1 %fusion.19 = f32[256,1024]{1,0:T(8,128)} fusion(bf16[2048,1024]{1,0:T(8,128)(2,1)} %param.26, f32[256,2048]{1,0:T(8,128)} %all-reduce.2.cloned.1.call-done, f32[2048]{0:T(1024)S(1)} %copy-done.10, f32[256]{0:T(256)S(1)} %bitcast.93, f32[256]{0:T(256)S(1)} %bitcast.94, f32[256]{0:T(256)S(1)} %bitcast.88, f32[256]{0:T(256)S(1)} %bitcast.89, ...), kind=kOutput, calls=%fused_computation.12 | convolution fusion | flops 1083179008 | bytes 7372800 | tf_op jit(solution)/shard_map/dot_general | solution.py:155
  358.2 0.0 reduce-scatter.8.cloned.1.call-update
  358.3 91.5 %reduce-scatter.8.cloned.1.call-done = f32[8,1024]{1,0:T(8,128)} async-done(((f32[256,1024]{1,0:T(8,128)}), f32[8,1024]{1,0:T(8,128)}) %reduce-scatter.8.cloned.1.call-update) | async-done | bytes 32784 | tf_op jit(solution)/shard_map/reduce_scatter | solution.py:154
  449.8 1.4 add_convert_fusion
  (24 shorter events, 0.1 us)
Async XLA Ops:
  6.5 113.8 %copy-start = (bf16[8,1,1024,128]{3,2,1,0:T(8,128)(2,1)S(1)}, bf16[8,1,1024,128]{3,2,1,0:T(8,128)(2,1)}, u32[]{:S(2)}) copy-start(bf16[8,1,1024,128]{3,2,1,0:T(8,128)(2,1)} %param.21) | copy-start | bytes 6291460
  6.5 27.1 %copy-start.4 = (bf16[256,128]{1,0:T(8,128)(2,1)S(1)}, bf16[256,128]{1,0:T(8,128)(2,1)}, u32[]{:S(2)}) copy-start(bf16[256,128]{1,0:T(8,128)(2,1)} %param.19) | copy-start | bytes 196612
  6.5 27.3 %copy-start.5 = (bf16[256,128]{1,0:T(8,128)(2,1)S(1)}, bf16[256,128]{1,0:T(8,128)(2,1)}, u32[]{:S(2)}) copy-start(bf16[256,128]{1,0:T(8,128)(2,1)} %param.18) | copy-start | bytes 196612
  6.5 111.7 %reduce-scatter.4.cloned.1.call-start = ((), (), s32[]{:S(2)}) async-start(), calls=%async_computation.5 | async-start | bytes 1351680 | tf_op jit(solution)/shard_map/reduce_scatter | solution.py:103
  33.9 1.5 copy-start.9
  35.3 182.4 %reduce-scatter.6.cloned.1.call-start = ((), (), s32[]{:S(2)}) async-start(), calls=%async_computation.6 | async-start | bytes 294912 | tf_op jit(solution)/shard_map/reduce_scatter | solution.py:139
  118.2 3.8 copy-start.1
  121.1 48.0 %copy-start.3 = (bf16[1024,256]{1,0:T(8,128)(2,1)S(1)}, bf16[1024,256]{1,0:T(8,128)(2,1)}, u32[]{:S(2)}) copy-start(bf16[1024,256]{1,0:T(8,128)(2,1)} %param.20) | copy-start | bytes 1572868
  122.0 65.6 %copy-start.2 = (bf16[8,8192]{1,0:T(8,128)(2,1)S(1)}, bf16[8,8192]{1,0:T(8,128)(2,1)}, u32[]{:S(2)}) copy-start(bf16[8,8192]{1,0:T(8,128)(2,1)} %param.15) | copy-start | bytes 393220
  187.6 164.5 %all-reduce.2.cloned.1.call-start = ((), (), s32[]{:S(2)}) async-start(), calls=%async_computation.7 | async-start | bytes 4194304 | tf_op jit(solution)/shard_map/psum | solution.py:151
  275.1 0.7 copy-start.6
  275.1 0.7 copy-start.7
  275.1 77.0 %copy-start.10 = (f32[2048]{0:T(1024)S(1)}, f32[2048]{0:T(1024)}, u32[]{:S(2)}) copy-start(f32[2048]{0:T(1024)} %param.25) | copy-start | bytes 24580
  275.1 174.7 %reduce-scatter.8.cloned.1.call-start = ((), (), s32[]{:S(2)}) async-start(), calls=%async_computation.8 | async-start | bytes 1081344 | tf_op jit(solution)/shard_map/reduce_scatter | solution.py:154
  352.1 97.7 %copy-start.8 = (f32[1024]{0:T(1024)S(1)}, f32[1024]{0:T(1024)}, u32[]{:S(2)}) copy-start(f32[1024]{0:T(1024)} %param.27) | copy-start | bytes 12292
Sparse Core Ops, SparseCore 0:
  35.4 82.7 reduce-scatter.3
  187.7 29.9 reduce-scatter.5
  275.2 76.8 all-reduce.1
  358.4 91.3 reduce-scatter.7
where the time goes:
time: 459 us; the launch traced here: 458 us
  waiting for transfers between devices  281 us (61%)
  blocking collectives  140 us (31%)
  matrix products  14.3 us (3%)
  between operations  13.3 us (3%)
  other arithmetic  6.94 us (2%)
    reduce_scatter x1, waiting for transfers between devices, on_device(): lax.psum_scatter(jnp.dot(row_block, w_dec, preferred_element_type=jnp.flo...  91.5 us
    reduce_scatter x1, waiting for transfers between devices, on_device(): lax.psum_scatter(jnp.concatenate([jnp.dot(row_block, w_query, preferred_e...  82.7 us
    psum x1, waiting for transfers between devices, on_device(): summed_pre = lax.psum(partial_pre, 'narrow')  76.3 us
    all_gather x1, blocking collectives, on_device(): lax.all_gather(hidden, 'wide', axis=0, tiled=True)  51.9 us
    all_gather x1, blocking collectives, on_device(): lax.all_gather(attended, 'wide', axis=0, tiled=True)  46.6 us
    reduce_scatter x1, waiting for transfers between devices, on_device(): lax.psum_scatter(by_row, 'narrow', scatter_dimension=1, tiled=True)  30 us
    all_to_all x1, blocking collectives, on_device(): lax.all_to_all(normalized_rows, 'wide', split_axis=1, concat_axis=0, tile...  23.5 us
    all_to_all x1, blocking collectives, on_device(): lax.all_to_all(partial_out, 'wide', split_axis=0, concat_axis=1, tiled=True)  18.1 us
  transfers between devices with their start and end apart: 4, of which 4 were waited for; matrix products, arithmetic and copies ran while one was open for 0% of the time, Pallas kernels for 0%

commit v1 on v0

--- a/solution.py
+++ b/solution.py
@@ -24,6 +24,20 @@
         [first_half * cosine - second_half * sine, second_half * cosine + first_half * sine],
         axis=-1,
     )
+
+
+def scatter_sum(partial, axis_name, groups, dim):
+    shape = partial.shape
+    pieces = partial.reshape(shape[:dim] + (groups, shape[dim] // groups) + shape[dim + 1 :])
+    pieces = jnp.moveaxis(pieces, dim, 0)
+    moved = lax.all_to_all(pieces, axis_name, split_axis=0, concat_axis=0, tiled=True)
+    return jnp.sum(moved, axis=0)
+
+
+def gather_rows(block, axis_name, groups):
+    copies = jnp.broadcast_to(block[None], (groups,) + block.shape)
+    moved = lax.all_to_all(copies, axis_name, split_axis=0, concat_axis=0, tiled=True)
+    return moved.reshape((groups * block.shape[0],) + block.shape[1:])
 
 
 def clamp_latents(pre_acts, latent_first, clamp_index, clamp_value):
@@ -100,7 +114,9 @@
     query_width = w_query.shape[1]
     key_width = key_projection_weight.shape[1]
     row_block = by_feature
-    projected = lax.psum_scatter(
+    wide_size = lax.axis_size("wide")
+    narrow_size = lax.axis_size("narrow")
+    projected = scatter_sum(
         jnp.concatenate(
             [
                 jnp.dot(row_block, w_query, preferred_element_type=jnp.float32),
@@ -110,8 +126,8 @@
             axis=1,
         ),
         "wide",
-        scatter_dimension=0,
-        tiled=True,
+        wide_size,
+        0,
     )
     heads_here = query_width // HEAD_WIDTH
     kv_here = key_width // HEAD_WIDTH
@@ -131,31 +147,38 @@
     )
     attended = attend(queries, key_new, value_new, cache_keys, stored_values, lengths)
     partial_out = jnp.dot(
-        lax.all_gather(attended, "wide", axis=0, tiled=True),
+        gather_rows(attended, "wide", wide_size),
         w_out,
         preferred_element_type=jnp.float32,
     )
     by_row = lax.all_to_all(partial_out, "wide", split_axis=0, concat_axis=1, tiled=True)
-    head_total = lax.psum_scatter(by_row, "narrow", scatter_dimension=1, tiled=True)
+    head_total = scatter_sum(by_row, "narrow", narrow_size, 1)
     width_here = w_enc.shape[0]
     narrow_index = lax.axis_index("narrow")
     own_stream = lax.dynamic_slice_in_dim(stream, narrow_index * width_here, width_here, 1)
     hidden = (own_stream + head_total).astype(jnp.bfloat16)
     partial_pre = jnp.dot(
-        lax.all_gather(hidden, "wide", axis=0, tiled=True),
+        gather_rows(hidden, "wide", wide_size),
         w_enc,
         preferred_element_type=jnp.float32,
     )
     latents_here = w_enc.shape[1]
     latent_first = lax.axis_index("wide") * latents_here
-    summed_pre = lax.psum(partial_pre, "narrow")
-    activations = clamp_latents(summed_pre + b_enc[None, :], latent_first, clamp_index, clamp_value)
+    summed_pre = scatter_sum(partial_pre, "narrow", narrow_size, 0)
+    rows_here = summed_pre.shape[0]
+    own_clamps = lax.dynamic_slice_in_dim(clamp_index, narrow_index * rows_here, rows_here, 0)
+    own_values = lax.dynamic_slice_in_dim(clamp_value, narrow_index * rows_here, rows_here, 0)
+    activations = gather_rows(
+        clamp_latents(summed_pre + b_enc[None, :], latent_first, own_clamps, own_values),
+        "narrow",
+        narrow_size,
+    )
     row_block = activations
-    rebuilt = lax.psum_scatter(
+    rebuilt = scatter_sum(
         jnp.dot(row_block, w_dec, preferred_element_type=jnp.float32),
         "wide",
-        scatter_dimension=0,
-        tiled=True,
+        wide_size,
+        0,
     )
     return (rebuilt + b_dec[None, :]).astype(jnp.bfloat16)
 

time: 459 us -> 241 us (0.53)
  waiting for transfers between devices: 281 us -> 64.5 us
  between operations: 13.3 us -> 0.3 us
  starting transfers between devices: 0.13 us -> 12.2 us
    reduce_scatter x3 -> x0, waiting for transfers between devices: 204 us -> none  [the longest x1 91.5 us: on_device(): lax.psum_scatter(jnp.dot(row_block, w_dec, preferred_element_type=jnp.flo...]
    all_to_all x0 -> x4, blocking collectives: none -> 101 us  [the longest x3 65.9 us: gather_rows(): lax.all_to_all(copies, axis_name, split_axis=0, concat_axis=0, tiled=True)]
    all_gather x2 -> x0, blocking collectives: 98.5 us -> none  [the longest x1 51.9 us: on_device(): lax.all_gather(hidden, 'wide', axis=0, tiled=True)]
    psum x1 -> x0, waiting for transfers between devices: 76.3 us -> none  [on_device(): summed_pre = lax.psum(partial_pre, 'narrow')]
    all_to_all x0 -> x3, waiting for transfers between devices: none -> 64.5 us  [scatter_sum(): lax.all_to_all(pieces, axis_name, split_axis=0, concat_axis=0, tiled=True)]
    all_to_all x0 -> x3, starting transfers between devices: none -> 12.2 us  [scatter_sum(): lax.all_to_all(pieces, axis_name, split_axis=0, concat_axis=0, tiled=True)]
  transfers between devices with their start and end apart: 4 -> 3, of which waited for: 4 -> 3; matrix products, arithmetic and copies ran while one was open for 0% -> 0% of each run, Pallas kernels for 0% -> 0%
where the time goes in v1:
time: 241 us; the launch traced here: 240 us
  blocking collectives  142 us (59%)
  waiting for transfers between devices  64.5 us (27%)
  starting transfers between devices  12.2 us (5%)
  matrix products  11.6 us (5%)
  other arithmetic  6.92 us (3%)
    all_to_all x3, blocking collectives, gather_rows(): lax.all_to_all(copies, axis_name, split_axis=0, concat_axis=0, tiled=True)  65.9 us
    all_to_all x3, waiting for transfers between devices, scatter_sum(): lax.all_to_all(pieces, axis_name, split_axis=0, concat_axis=0, tiled=True)  64.5 us
    all_to_all x1, blocking collectives, scatter_sum(): lax.all_to_all(pieces, axis_name, split_axis=0, concat_axis=0, tiled=True)  35.5 us
    all_to_all x1, blocking collectives, on_device(): lax.all_to_all(normalized_rows, 'wide', split_axis=1, concat_axis=0, tile...  23.5 us
    all_to_all x1, blocking collectives, on_device(): lax.all_to_all(partial_out, 'wide', split_axis=0, concat_axis=1, tiled=True)  17.5 us
    all_to_all x3, starting transfers between devices, scatter_sum(): lax.all_to_all(pieces, axis_name, split_axis=0, concat_axis=0, tiled=True)  12.2 us
  transfers between devices with their start and end apart: 3, of which 3 were waited for; matrix products, arithmetic and copies ran while one was open for 0% of the time, Pallas kernels for 0%

profile of v1, /device:TPU:1, one launch (start us, length us, event | category | flops | bytes accessed | tf_op | source)
XLA Modules:
  0.0 240.2 jit_solution(5929499355266509744)
XLA Ops:
  0.0 1.2 multiply_reduce_fusion
  1.3 1.0 multiply_convert_fusion
  2.3 23.5 %all_to_all.67 = bf16[8,32,256]{2,0,1:T(8,128)(2,1)S(1)} all-to-all(bf16[8,32,256]{2,0,1:T(8,128)(2,1)S(1)} %bitcast.105), channel_id=1, replica_groups=mesh['wide'=32,'narrow'=8] {'wide'}, dimensions={1} | all-to-all | bytes 262144 | tf_op jit(solution)/shard_map/all_to_all | solution.py:113
  25.8 1.3 fusion.30
  27.2 0.2 fusion.26
  27.3 0.2 fusion.28
  27.5 0.0 copy-start.9
  27.5 1.2 maximum_bitcast_fusion
  28.7 3.8 %all-to-all-start.1 = ((f32[32,8,1280]{2,1,0:T(8,128)}), f32[32,8,1280]{2,1,0:T(8,128)S(1)}, u32[]{:S(2)}, u32[]{:S(2)}) async-start(f32[32,8,1280]{2,1,0:T(8,128)} %maximum_bitcast_fusion), calls=%async_computation.1 | async-start | bytes 2621440 | tf_op jit(solution)/shard_map/all_to_all | solution.py:33
  32.5 0.1 iota_compare_fusion
  32.6 0.1 multiply_cosine_fusion.1
  32.7 33.5 %all-to-all-done.1 = f32[32,8,1280]{2,1,0:T(8,128)S(1)} async-done(((f32[32,8,1280]{2,1,0:T(8,128)}), f32[32,8,1280]{2,1,0:T(8,128)S(1)}, u32[]{:S(2)}, u32[]{:S(2)}) %all-to-all-start.1) | async-done | bytes 1310752 | tf_op jit(solution)/shard_map/all_to_all | solution.py:33
  66.3 0.1 reduce_sum.55
  66.3 0.0 copy-start.1
  66.4 0.1 fusion.47
  66.5 0.1 maximum_bitcast_fusion.1
  66.6 0.1 subtract_convert_fusion
  66.7 0.2 fusion.42
  66.9 0.8 fusion.51
  67.6 0.2 fusion.25
  67.9 0.1 copy-done.1
  67.9 0.4 fusion.20
  68.4 0.1 broadcast_in_dim.135
  68.4 24.3 %all_to_all.68 = bf16[32,8,1024]{2,1,0:T(8,128)(2,1)S(1)} all-to-all(bf16[32,8,1024]{2,1,0:T(8,128)(2,1)S(1)} %broadcast_in_dim.135), channel_id=1, replica_groups=mesh['wide'=32,'narrow'=8] {'wide'}, dimensions={0} | all-to-all | bytes 1048576 | tf_op jit(solution)/shard_map/all_to_all | solution.py:39
  92.8 0.3 fusion.23
  93.1 17.5 %all_to_all.69 = f32[32,8,256]{2,1,0:T(8,128)S(1)} all-to-all(f32[32,8,256]{2,1,0:T(8,128)S(1)} %fusion.23), channel_id=1, replica_groups=mesh['wide'=32,'narrow'=8] {'wide'}, dimensions={0} | all-to-all | bytes 524288 | tf_op jit(solution)/shard_map/all_to_all | solution.py:154
  110.6 0.1 copy.23
  110.7 0.1 reshape.607
  110.8 0.8 copy.24
  111.6 4.0 %all-to-all-start.4 = ((f32[8,8,1024]{2,1,0:T(8,128)}), f32[8,8,1024]{2,1,0:T(8,128)S(1)}, u32[]{:S(2)}, u32[]{:S(2)}) async-start(f32[8,8,1024]{2,1,0:T(8,128)} %copy.24), calls=%async_computation.4 | async-start | bytes 524288 | tf_op jit(solution)/shard_map/all_to_all | solution.py:33
  115.6 6.1 %all-to-all-done.4 = f32[8,8,1024]{2,1,0:T(8,128)S(1)} async-done(((f32[8,8,1024]{2,1,0:T(8,128)}), f32[8,8,1024]{2,1,0:T(8,128)S(1)}, u32[]{:S(2)}, u32[]{:S(2)}) %all-to-all-start.4) | async-done | bytes 262176 | tf_op jit(solution)/shard_map/all_to_all | solution.py:33
  121.8 0.1 broadcast_in_dim.136
  121.8 23.8 %all_to_all.70 = bf16[32,8,1024]{2,1,0:T(8,128)(2,1)S(1)} all-to-all(bf16[32,8,1024]{2,1,0:T(8,128)(2,1)S(1)} %broadcast_in_dim.136), channel_id=1, replica_groups=mesh['wide'=32,'narrow'=8] {'wide'}, dimensions={0} | all-to-all | bytes 1048576 | tf_op jit(solution)/shard_map/all_to_all | solution.py:39
  145.6 4.8 %fusion.2 = f32[8,32,2048]{2,1,0:T(8,128)} fusion(bf16[8,32,1024]{2,1,0:T(8,128)(2,1)S(1)} %bitcast.101, bf16[1024,2048]{1,0:T(8,128)(2,1)} %param.24), kind=kOutput, calls=%fused_computation.2 | convolution fusion | flops 1073741824 | bytes 6815744 | tf_op jit(solution)/shard_map/dot_general | solution.py:160
  150.4 4.5 %all-to-all-start.6 = ((f32[8,32,2048]{2,1,0:T(8,128)}), f32[8,32,2048]{2,1,0:T(8,128)}, u32[]{:S(2)}, u32[]{:S(2)}) async-start(f32[8,32,2048]{2,1,0:T(8,128)} %fusion.2), calls=%async_computation.6 | async-start | bytes 4194304 | tf_op jit(solution)/shard_map/all_to_all | solution.py:33
  154.9 0.0 copy-start.6
  154.9 0.8 constant_dynamic-slice_fusion
  155.7 0.1 constant_dynamic-slice_fusion.1
  155.8 24.8 %all-to-all-done.6 = f32[8,32,2048]{2,1,0:T(8,128)} async-done(((f32[8,32,2048]{2,1,0:T(8,128)}), f32[8,32,2048]{2,1,0:T(8,128)}, u32[]{:S(2)}, u32[]{:S(2)}) %all-to-all-start.6) | async-done | bytes 2097184 | tf_op jit(solution)/shard_map/all_to_all | solution.py:33
  180.6 1.7 reduce_sum.58
  182.3 0.3 select_convert_fusion
  182.6 0.1 broadcast_in_dim.137
  182.7 17.8 %all_to_all.71 = bf16[8,32,2048]{2,1,0:T(8,128)(2,1)S(1)} all-to-all(bf16[8,32,2048]{2,1,0:T(8,128)(2,1)S(1)} %broadcast_in_dim.137), channel_id=1, replica_groups=mesh['wide'=32,'narrow'=8] {'narrow'}, dimensions={0} | all-to-all | bytes 2097152 | tf_op jit(solution)/shard_map/all_to_all | solution.py:39
  200.5 3.5 %fusion = f32[32,8,1024]{2,1,0:T(8,128)S(1)} fusion(bf16[32,8,2048]{2,1,0:T(8,128)(2,1)S(1)} %bitcast.102, bf16[2048,1024]{1,0:T(8,128)(2,1)} %param.26), kind=kOutput, calls=%fused_computation | convolution fusion | flops 1073741824 | bytes 6291456 | tf_op jit(solution)/shard_map/dot_general | solution.py:178
  204.0 0.0 copy-start.7
  204.0 35.5 %all_to_all.72 = f32[32,8,1024]{2,1,0:T(8,128)S(1)} all-to-all(f32[32,8,1024]{2,1,0:T(8,128)S(1)} %fusion), channel_id=1, replica_groups=mesh['wide'=32,'narrow'=8] {'wide'}, dimensions={0} | all-to-all | bytes 2097152 | tf_op jit(solution)/shard_map/all_to_all | solution.py:33
  239.5 0.1 reduce_sum.59
  239.6 0.6 add_convert_fusion
  (31 shorter events, 0.2 us)
Async XLA Ops:
  0.0 66.9 %copy-start = (bf16[8,1,1024,128]{3,2,1,0:T(8,128)(2,1)S(1)}, bf16[8,1,1024,128]{3,2,1,0:T(8,128)(2,1)}, u32[]{:S(2)}) copy-start(bf16[8,1,1024,128]{3,2,1,0:T(8,128)(2,1)} %param.21) | copy-start | bytes 6291460
  0.0 27.1 %copy-start.4 = (bf16[256,128]{1,0:T(8,128)(2,1)S(1)}, bf16[256,128]{1,0:T(8,128)(2,1)}, u32[]{:S(2)}) copy-start(bf16[256,128]{1,0:T(8,128)(2,1)} %param.19) | copy-start | bytes 196612
  0.0 27.3 %copy-start.5 = (bf16[256,128]{1,0:T(8,128)(2,1)S(1)}, bf16[256,128]{1,0:T(8,128)(2,1)}, u32[]{:S(2)}) copy-start(bf16[256,128]{1,0:T(8,128)(2,1)} %param.18) | copy-start | bytes 196612
  27.5 5.0 %copy-start.9 = (s32[8]{0:T(128)S(1)}, s32[8]{0:T(128)}, u32[]{:S(2)}) copy-start(s32[8]{0:T(128)} %param.23) | copy-start | bytes 100
  28.7 37.6 %all-to-all-start.1 = ((f32[32,8,1280]{2,1,0:T(8,128)}), f32[32,8,1280]{2,1,0:T(8,128)S(1)}, u32[]{:S(2)}, u32[]{:S(2)}) async-start(f32[32,8,1280]{2,1,0:T(8,128)} %maximum_bitcast_fusion), calls=%async_computation.1 | async-start | bytes 2621440 | tf_op jit(solution)/shard_map/all_to_all | solution.py:33
  66.3 1.6 copy-start.1
  67.6 25.1 %copy-start.3 = (bf16[1024,256]{1,0:T(8,128)(2,1)S(1)}, bf16[1024,256]{1,0:T(8,128)(2,1)}, u32[]{:S(2)}) copy-start(bf16[1024,256]{1,0:T(8,128)(2,1)} %param.20) | copy-start | bytes 1572868
  92.8 22.8 %copy-start.2 = (bf16[8,8192]{1,0:T(8,128)(2,1)S(1)}, bf16[8,8192]{1,0:T(8,128)(2,1)}, u32[]{:S(2)}) copy-start(bf16[8,8192]{1,0:T(8,128)(2,1)} %param.15) | copy-start | bytes 393220
  111.6 10.1 %all-to-all-start.4 = ((f32[8,8,1024]{2,1,0:T(8,128)}), f32[8,8,1024]{2,1,0:T(8,128)S(1)}, u32[]{:S(2)}, u32[]{:S(2)}) async-start(f32[8,8,1024]{2,1,0:T(8,128)} %copy.24), calls=%async_computation.4 | async-start | bytes 524288 | tf_op jit(solution)/shard_map/all_to_all | solution.py:33
  150.4 5.3 %copy-start.8 = (s32[256,8]{0,1:T(8,128)S(1)}, s32[256,8]{0,1:T(8,128)}, u32[]{:S(2)}) copy-start(s32[256,8]{0,1:T(8,128)} %param.28) | copy-start | bytes 24580
  150.4 30.2 %all-to-all-start.6 = ((f32[8,32,2048]{2,1,0:T(8,128)}), f32[8,32,2048]{2,1,0:T(8,128)}, u32[]{:S(2)}, u32[]{:S(2)}) async-start(f32[8,32,2048]{2,1,0:T(8,128)} %fusion.2), calls=%async_computation.6 | async-start | bytes 4194304 | tf_op jit(solution)/shard_map/all_to_all | solution.py:33
  154.9 27.4 %copy-start.6 = (f32[2048]{0:T(1024)S(1)}, f32[2048]{0:T(1024)}, u32[]{:S(2)}) copy-start(f32[2048]{0:T(1024)} %param.25) | copy-start | bytes 24580
  204.0 35.6 %copy-start.7 = (f32[1024]{0:T(1024)S(1)}, f32[1024]{0:T(1024)}, u32[]{:S(2)}) copy-start(f32[1024]{0:T(1024)} %param.27) | copy-start | bytes 12292
